TPU v7x, 256 devices: a whole 4x4x8 slice. The times are simulated.
256 devices in a mesh: wide: 32 (over x, y, core), blk: 8 (over z).
Axes of the slice: x: 4, y: 4, z: 8, core: 2. Of those that a mesh axis runs over, the one named last changes fastest.
Arguments:
- tokens: bfloat16 [1024, 8192], P('wide', 'blk'), may hold values from -6 to 6
- target: bfloat16 [1024, 8192], P('wide', 'blk'), may hold values from -3 to 3
- probe_vector: float32 [8192], P('blk'), may hold values from -12 to 12
- weight_in: bfloat16 [256, 8, 2, 128, 128], P('wide', 'blk'), may hold values from -0.375 to 0.375
- weight_out: bfloat16 [256, 8, 2, 128, 128], P('wide', 'blk'), may hold values from -0.09375 to 0.09375
- slot_rows: int32 [256, 8, 2], P('wide', 'blk'), may hold values from 0 to 7, as said below
- slot_count: int32 [256, 8], P('wide', 'blk'), may hold values from 0 to 2, as said below
Outputs:
- outputs: bfloat16 [1024, 8192], P('wide', 'blk')
- token_grad: bfloat16 [1024, 8192], P('wide', 'blk')
- grad_in: float32 [256, 8, 2, 128, 128], P('wide', 'blk')
- grad_out: float32 [256, 8, 2, 128, 128], P('wide', 'blk')
Inputs may be any that keep to these rules, and one draw needn't show every extreme that they name: `slot_rows`: the 2 entries of one (j, g) are distinct feature blocks of the row group. `slot_count`: every hidden block column has 2 used slots in at least one row group.
All inputs are finite; a program needn't handle non-finite values.
Results may differ from a plain program's by a relative error of at most 0.033.
Values may be sent and summed in bfloat16 or wider, within the bound.
No kernel may reach another device: no remote copies, remote signals or barrier semaphores. Data moves between devices by JAX's collectives and lax.ppermute only.
A program may use at most 64 MiB of HBM per device.

v0:
```python
import jax
import jax.numpy as jnp
from jax import lax
from jax.sharding import Mesh, PartitionSpec as P

WIDE = ("chip", "core")


def activate(value):
    return jax.nn.gelu(value, approximate=True)


def activate_slope(value):
    return jax.jvp(activate, (value,), (jnp.ones_like(value),))[1]


def spread_tiles(tiles, row_index, feature_blocks):
    rows = lax.broadcasted_iota(jnp.int32, (feature_blocks,) + row_index.shape, 0)
    hit = rows == row_index[None]
    zero = jnp.zeros((), tiles.dtype)
    dense = jnp.where(hit[:, :, 0, None, None], tiles[None, :, 0], zero)
    for slot in range(1, row_index.shape[1]):
        dense = dense + jnp.where(hit[:, :, slot, None, None], tiles[None, :, slot], zero)
    return jnp.transpose(dense, (0, 2, 1, 3))


def pick_tiles(dense, row_index):
    feature_blocks = dense.shape[0]
    rows = lax.broadcasted_iota(jnp.int32, (feature_blocks,) + row_index.shape, 0)
    hit = rows == row_index[None]
    by_col = jnp.transpose(dense, (0, 2, 1, 3))
    chosen = jnp.where(hit[:, :, :, None, None], by_col[:, :, None], 0.0)
    return jnp.sum(chosen, axis=0)


def group_size(axis):
    if isinstance(axis, tuple):
        size = 1
        for name in axis:
            size *= lax.axis_size(name)
        return size
    return lax.axis_size(axis)


def butterfly_sum(value, axis):
    size = group_size(axis)
    step = 1
    while step < size:
        value = value + lax.ppermute(value, axis, [(i, i ^ step) for i in range(size)])
        step *= 2
    return value


def gather_rows(value):
    chips = lax.axis_size("chip")
    spread = jnp.broadcast_to(value[None], (chips,) + value.shape)
    mine = lax.all_to_all(spread, "chip", 0, 0, tiled=False)
    other = lax.ppermute(mine, "core", [(0, 1), (1, 0)])
    first = lax.axis_index("core") == 0
    pair = jnp.stack([jnp.where(first, mine, other), jnp.where(first, other, mine)], 1)
    return pair.reshape((-1,) + value.shape[1:])


def pair_rows(left, product):
    chips = lax.axis_size("chip")
    parts = left.reshape((chips, 2, -1) + left.shape[1:])
    first = lax.axis_index("core") == 0
    keep_in = jnp.where(first, parts[:, 0], parts[:, 1]).reshape((-1,) + left.shape[1:])
    give_in = jnp.where(first, parts[:, 1], parts[:, 0]).reshape((-1,) + left.shape[1:])
    give = product(give_in).astype(jnp.bfloat16)
    got = lax.ppermute(give, "core", [(0, 1), (1, 0)])
    keep = product(keep_in).astype(jnp.bfloat16)
    pair = keep.astype(jnp.float32) + got.astype(jnp.float32)
    return pair.astype(jnp.bfloat16).reshape((chips, -1) + pair.shape[1:])


def sum_rows(left, product):
    received = lax.all_to_all(pair_rows(left, product), "chip", 0, 0, tiled=False)
    return jnp.sum(received.astype(jnp.float32), axis=0)


def split_three(value):
    high = value.astype(jnp.bfloat16)
    rest = value - high.astype(jnp.float32)
    middle = rest.astype(jnp.bfloat16)
    low = (rest - middle.astype(jnp.float32)).astype(jnp.bfloat16)
    return jnp.stack([high, middle, low])


def join_three(pieces):
    pieces = pieces.astype(jnp.float32)
    return pieces[..., 0] + pieces[..., 1] + pieces[..., 2]


def with_row(rows, pieces):
    extra = jnp.zeros((1, rows.shape[1]), rows.dtype).at[0, : pieces.shape[0]].set(pieces)
    return jnp.concatenate([rows, extra], axis=0)


def body(tokens, target, probe_vector, weight_in, weight_out, slot_rows, slot_count):
    columns, unit, slots, block, width_two = weight_in.shape
    features = tokens.shape[1]
    feature_blocks = features // block
    hidden_width = columns * block
    row_index = slot_rows[:, 0]
    in_use = lax.broadcasted_iota(jnp.int32, (columns, slots), 1) < slot_count[:, 0][:, None]
    mask_low = in_use.astype(jnp.bfloat16)[:, :, None, None]
    mask_full = in_use.astype(jnp.float32)[:, :, None, None]
    tiles_in = weight_in[:, 0] * mask_low
    tiles_out = weight_out[:, 0] * mask_low
    chosen = jnp.take(
        probe_vector.reshape(feature_blocks, block), row_index.reshape(-1), axis=0
    ).reshape(columns, slots, block)
    image_part = jnp.einsum(
        "jsk,jskn->jn", chosen, tiles_in.astype(jnp.float32), precision=lax.Precision.HIGHEST
    )
    x_full = gather_rows(tokens)
    image_and_norm = butterfly_sum(
        jnp.concatenate([image_part.reshape(-1), jnp.sum(probe_vector * probe_vector)[None]]), "blk"
    )
    image = image_and_norm[:-1].reshape(image_part.shape)
    norm_probe = image_and_norm[-1]
    norm_image = butterfly_sum(jnp.sum(image * image)[None], WIDE)[0]
    spectral = jnp.sqrt(norm_image / norm_probe)
    w1 = spread_tiles(tiles_in, row_index, feature_blocks).reshape(features, hidden_width)
    w2 = jnp.transpose(spread_tiles(tiles_out, row_index, feature_blocks), (2, 1, 0, 3)).reshape(
        hidden_width, features
    )
    pre_part = jnp.dot(x_full, w1, preferred_element_type=jnp.float32)
    pre_own = lax.psum_scatter(
        pre_part.astype(jnp.bfloat16), "blk", scatter_dimension=0, tiled=True
    ).astype(jnp.float32)
    pre_own, spectral = lax.optimization_barrier((pre_own, spectral))
    hidden_own = pre_own / spectral
    active_own = activate(hidden_own).astype(jnp.bfloat16)
    active_full = lax.all_gather(active_own, "blk", axis=0, tiled=True)
    outputs = sum_rows(
        active_full, lambda rows: jnp.dot(rows, w2, preferred_element_type=jnp.float32)
    ).astype(jnp.bfloat16)
    residual = (outputs.astype(jnp.float32) - target.astype(jnp.float32)).astype(jnp.bfloat16)
    error_full = gather_rows(residual)
    back_part = lax.dot_general(
        error_full, w2, (((1,), (1,)), ((), ())), preferred_element_type=jnp.float32
    )
    back_own = lax.psum_scatter(
        back_part.astype(jnp.bfloat16), "blk", scatter_dimension=0, tiled=True
    ).astype(jnp.float32)
    g2 = lax.dot_general(
        error_full, active_full, (((0,), (0,)), ((), ())), preferred_element_type=jnp.float32
    )
    grad_out = pick_tiles(g2.reshape(feature_blocks, block, columns, block), row_index) * mask_full
    grad_out = jnp.transpose(grad_out, (0, 1, 3, 2))
    back_own, grad_out = lax.optimization_barrier((back_own, grad_out))
    slope_own = (back_own * activate_slope(hidden_own)).astype(jnp.bfloat16)
    curvature_part = jnp.sum(slope_own.astype(jnp.float32) * pre_own)
    slope_rows = lax.all_gather(
        with_row(slope_own, split_three(curvature_part)), "blk", axis=0, tiled=False
    )
    slope_full = slope_rows[:, :-1].reshape(-1, slope_own.shape[1])
    curvature_blk = jnp.sum(join_three(slope_rows[:, -1, :3]))
    in_rows = pair_rows(
        slope_full,
        lambda rows: lax.dot_general(
            rows, w1, (((1,), (1,)), ((), ())), preferred_element_type=jnp.float32
        ),
    )
    curvature_chip = curvature_blk + lax.ppermute(curvature_blk, "core", [(0, 1), (1, 0)])
    extra = (
        jnp.zeros((in_rows.shape[0], 1, features), jnp.bfloat16)
        .at[:, 0, :3]
        .set(split_three(curvature_chip)[None])
    )
    received = lax.all_to_all(jnp.concatenate([in_rows, extra], axis=1), "chip", 0, 0, tiled=False)
    token_grad = (jnp.sum(received[:, :-1].astype(jnp.float32), axis=0) / spectral).astype(
        jnp.bfloat16
    )
    curvature = jnp.sum(join_three(received[:, -1, :3]))
    g1 = lax.dot_general(
        x_full, slope_full, (((0,), (0,)), ((), ())), preferred_element_type=jnp.float32
    )
    raw_in = pick_tiles(g1.reshape(feature_blocks, block, columns, block), row_index) * mask_full
    outer = jnp.einsum("jsk,jn->jskn", chosen, image) * mask_full
    grad_in = raw_in / spectral - curvature / (spectral**3 * norm_probe) * outer
    return (outputs, token_grad, grad_in[:, None], grad_out[:, None])


def solution(mesh):
    wide, blk = (mesh.shape["wide"], mesh.shape["blk"])
    split = Mesh(mesh.devices.reshape(wide // 2, 2, blk), ("chip", "core", "blk"))
    in_specs = (
        P(WIDE, "blk"),
        P(WIDE, "blk"),
        P("blk"),
        P(WIDE, "blk", None, None, None),
        P(WIDE, "blk", None, None, None),
        P(WIDE, "blk", None),
        P(WIDE, "blk"),
    )
    out_specs = (
        P(WIDE, "blk"),
        P(WIDE, "blk"),
        P(WIDE, "blk", None, None, None),
        P(WIDE, "blk", None, None, None),
    )
    return jax.shard_map(body, mesh=split, in_specs=in_specs, out_specs=out_specs, check_vma=False)
```

profile of v0, /device:TPU:32, one launch (start us, length us, event | category | flops | bytes accessed | tf_op | source)
XLA Modules:
  0.0 324.5 jit_solution(9153554988454920634)
XLA Ops:
  7.2 1.9 broadcast_in_dim.148
  9.1 7.0 %all-to-all-start = ((bf16[16,32,1024]{2,1,0:T(8,128)(2,1)}), bf16[16,32,1024]{2,1,0:T(8,128)(2,1)S(1)}, u32[]{:S(2)}, u32[]{:S(2)}) async-start(bf16[16,32,1024]{2,1,0:T(8,128)(2,1)} %broadcast_in_dim.148), calls=%async_computation | async-start | bytes 2097152 | tf_op jit(solution)/shard_map/all_to_all | solution.py:57
  16.3 17.6 %all-to-all-done = bf16[16,32,1024]{2,1,0:T(8,128)(2,1)S(1)} async-done(((bf16[16,32,1024]{2,1,0:T(8,128)(2,1)}), bf16[16,32,1024]{2,1,0:T(8,128)(2,1)S(1)}, u32[]{:S(2)}, u32[]{:S(2)}) %all-to-all-start) | async-done | bytes 1048608 | tf_op jit(solution)/shard_map/all_to_all | solution.py:57
  33.9 1.3 bitcast_multiply_fusion
  35.2 0.8 slice_bitcast_fusion.1
  37.2 0.9 copy-done.3
  38.1 0.6 copy-done
  38.8 3.7 %fusion.12 = bf16[1024,1024]{1,0:T(8,128)(2,1)} fusion(bf16[1024,1024]{1,0:T(8,128)(2,1)S(1)} %bitcast.166, bf16[128,8,8,128]{3,2,1,0:T(8,128)(2,1)S(1)} %bitcast.173), kind=kOutput, calls=%fused_computation.24 | convolution fusion | flops 2148532224 | bytes 6291456 | tf_op jit(solution)/shard_map/dot_general | solution.py:129
  44.7 0.7 pad_maximum_fusion.3
  45.6 3.5 %collective-permute-done.1 = f32[1025]{0:T(1024)S(1)} collective-permute-done((f32[1025]{0:T(1024)S(1)}, f32[1025]{0:T(1024)S(1)}, u32[]{:S(2)}, u32[]{:S(2)}) %collective-permute-start.1) | collective-permute-done | bytes 4132 | tf_op jit(solution)/shard_map/ppermute | solution.py:49
  49.1 0.6 fusion.63
  49.8 3.4 %collective-permute-start.2 = (f32[1025]{0:T(1024)S(1)}, f32[1025]{0:T(1024)S(1)}, u32[]{:S(2)}, u32[]{:S(2)}) collective-permute-start(f32[1025]{0:T(1024)S(1)} %fusion.63), channel_id=1, source_target_pairs={{0,2},{1,3},{2,0},{3,1},{4,6},{5,7},{6,4},{7,5},{8,10},{9,11},{10,... | collective-permute-start | bytes 12308 | tf_op jit(solution)/shard_map/ppermute | solution.py:49
  53.1 1.6 collective-permute-done.2
  54.8 6.0 %collective-permute-start.3 = (f32[1025]{0:T(1024)S(1)}, f32[1025]{0:T(1024)S(1)}, u32[]{:S(2)}, u32[]{:S(2)}) collective-permute-start(f32[1025]{0:T(1024)S(1)} %add.135), channel_id=1, source_target_pairs={{0,4},{1,5},{2,6},{3,7},{4,0},{5,1},{6,2},{7,3},{8,12},{9,13},{10,... | collective-permute-start | bytes 12308 | tf_op jit(solution)/shard_map/ppermute | solution.py:49
  60.8 1.7 collective-permute-done.3
  63.7 1.4 collective-permute-done.4
  66.3 2.0 collective-permute-start.5
  68.3 1.7 collective-permute-done.5
  70.7 2.1 collective-permute-start.6
  72.8 3.1 collective-permute-done.6
  76.6 1.4 collective-permute-start.7
  78.0 2.3 collective-permute-done.7
  80.9 2.0 collective-permute-start.8
  82.9 3.3 %collective-permute-done.8 = f32[1]{0:T(128)} collective-permute-done((f32[1]{0:T(128)}, f32[1]{0:T(128)}, u32[]{:S(2)}, u32[]{:S(2)}) %collective-permute-start.8) | collective-permute-done | bytes 36 | tf_op jit(solution)/shard_map/ppermute | solution.py:49
  87.6 1.0 convert_element_type.127
  88.6 0.9 multiply_convert_fusion
  90.4 38.5 %all-gather.5.cloned.1.call-done = bf16[1024,1024]{1,0:T(8,128)(2,1)} async-done(((bf16[128,1024]{1,0:T(8,128)(2,1)}), bf16[1024,1024]{1,0:T(8,128)(2,1)}) %all-gather.5.cloned.1.call-update) | async-done | bytes 2097168 | tf_op jit(solution)/shard_map/all_gather | solution.py:136
  128.9 1.7 broadcast_select_fusion.3
  130.6 1.2 fusion.33
  132.1 2.6 collective-permute-done.9
  134.8 1.3 add_convert_fusion.1
  136.0 24.1 %all_to_all.20 = bf16[16,32,1024]{2,1,0:T(8,128)(2,1)S(1)} all-to-all(bf16[16,32,1024]{2,1,0:T(8,128)(2,1)S(1)} %bitcast.189), channel_id=1, replica_groups=mesh['chip'=16,'core'=2,'blk'=8] {'chip'}, dimensions={0} | all-to-all | bytes 2097152 | tf_op jit(solution)/shard_map/all_to_all | solution.py:78
  160.6 19.5 %all_to_all.21 = bf16[16,32,1024]{2,1,0:T(8,128)(2,1)S(1)} all-to-all(bf16[16,32,1024]{2,1,0:T(8,128)(2,1)S(1)} %broadcast_in_dim.172), channel_id=1, replica_groups=mesh['chip'=16,'core'=2,'blk'=8] {'chip'}, dimensions={0} | all-to-all | bytes 2097152 | tf_op jit(solution)/shard_map/all_to_all | solution.py:57
  180.1 2.7 collective-permute-done.10
  183.4 1.4 copy-done.2
  184.8 0.7 copy-done.6
  185.4 3.7 %fusion.15 = bf16[1024,1024]{1,0:T(8,128)(2,1)} fusion(bf16[1024,1024]{1,0:T(8,128)(2,1)S(1)} %bitcast.170, bf16[128,8,8,128]{3,2,1,0:T(8,128)(2,1)S(1)} %bitcast.178), kind=kOutput, calls=%fused_computation.25 | convolution fusion | flops 2148532224 | bytes 6291456 | tf_op jit(solution)/shard_map/dot_general | solution.py:142
  190.0 0.7 copy-done.1
  190.8 2.6 copy.100
  193.3 4.1 %copy.88 = bf16[1024,1024]{1,0:T(8,128)(2,1)} copy(bf16[1024,1024]{0,1:T(8,128)(2,1)} %bitcast.171) | data formatting | bytes 4194304 | tf_op jit(solution)/shard_map/dot_general | solution.py:148
  197.5 4.0 %convolution_bitcast_fusion.1 = f32[8,8,128,128]{3,2,1,0:T(8,128)S(1)} fusion(bf16[8,128,1024,1]{2,1,3,0:T(8,128)(2,1)} %bitcast.181, bf16[8,128,1024,1]{2,1,0,3:T(8,128)(2,1)S(1)} %bitcast.180), kind=kOutput, calls=%fused_computation.4 | convolution fusion | flops 2147483648 | bytes 8388608 | tf_op jit(solution)/shard_map/dot_general | solution.py:148
  201.4 1.0 select_reduce_fusion.1
  202.4 1.1 multiply_bitcast_fusion
  203.5 23.0 %reduce-scatter.5.cloned.1.call-done = bf16[128,1024]{1,0:T(8,128)(2,1)} async-done(((bf16[1024,1024]{1,0:T(8,128)(2,1)}), bf16[128,1024]{1,0:T(8,128)(2,1)}) %reduce-scatter.5.cloned.1.call-update) | async-done | bytes 262160 | tf_op jit(solution)/shard_map/reduce_scatter | solution.py:145
  226.5 1.0 convert_element_type.138
  227.5 1.0 multiply_reduce_fusion
  229.8 0.7 broadcast_select_fusion.5
  230.5 0.7 fusion.54
  231.3 40.6 %all-gather.7.cloned.1.call-done = bf16[8,129,1024]{2,1,0:T(8,128)(2,1)} async-done(((bf16[1,129,1024]{2,1,0:T(8,128)(2,1)}), bf16[8,129,1024]{2,1,0:T(8,128)(2,1)}) %all-gather.7.cloned.1.call-update) | async-done | bytes 2113552 | tf_op jit(solution)/shard_map/all_gather | solution.py:156
  271.9 1.9 slice.145
  273.9 1.4 copy-done.4
  275.4 2.3 fusion.27
  277.6 0.7 slice.148
  279.6 1.1 collective-permute-done.12
  282.0 3.1 add_convert_fusion
  285.2 1.2 pad_maximum_fusion.2
  286.4 6.8 %all-to-all-start.3 = ((bf16[16,33,1024]{2,1,0:T(8,128)(2,1)}), bf16[16,33,1024]{2,1,0:T(8,128)(2,1)S(1)}, u32[]{:S(2)}, u32[]{:S(2)}) async-start(bf16[16,33,1024]{2,1,0:T(8,128)(2,1)} %pad_maximum_fusion.2), calls=%async_computation.5 | async-start | bytes 2621440 | tf_op jit(solution)/shard_map/all_to_all | solution.py:173
  293.2 4.0 %copy.91 = bf16[1024,1024]{1,0:T(8,128)(2,1)} copy(bf16[1024,1024]{0,1:T(8,128)(2,1)} %bitcast.167) | data formatting | bytes 4194304 | tf_op jit(solution)/shard_map/dot_general | solution.py:178
  297.9 2.5 copy.95
  300.4 2.6 copy.92
  303.0 4.6 %convolution_bitcast_fusion = f32[8,8,128,128]{3,2,1,0:T(8,128)S(1)} fusion(bf16[8,128,1024,1]{2,1,3,0:T(8,128)(2,1)} %bitcast.179, bf16[8,128,1024,1]{2,1,0,3:T(8,128)(2,1)} %bitcast.182), kind=kOutput, calls=%fused_computation.3 | convolution fusion | flops 2147483648 | bytes 8388608 | tf_op jit(solution)/shard_map/dot_general | solution.py:178
  307.6 1.0 select_reduce_fusion
  308.6 5.8 %all-to-all-done.3 = bf16[16,33,1024]{2,1,0:T(8,128)(2,1)S(1)} async-done(((bf16[16,33,1024]{2,1,0:T(8,128)(2,1)}), bf16[16,33,1024]{2,1,0:T(8,128)(2,1)S(1)}, u32[]{:S(2)}, u32[]{:S(2)}) %all-to-all-start.3) | async-done | bytes 1081376 | tf_op jit(solution)/shard_map/all_to_all | solution.py:173
  316.6 1.3 subtract_bitcast_fusion
  (85 shorter events, 10.8 us)
Async XLA Ops:
  7.2 9.0 %copy-start.13 = (s32[8,1]{0,1:T(1,128)S(1)}, s32[8,1]{0,1:T(1,128)}, u32[]{:S(2)}) copy-start(s32[8,1]{0,1:T(1,128)} %param.17) | copy-start | bytes 100
  9.1 24.7 %all-to-all-start = ((bf16[16,32,1024]{2,1,0:T(8,128)(2,1)}), bf16[16,32,1024]{2,1,0:T(8,128)(2,1)S(1)}, u32[]{:S(2)}, u32[]{:S(2)}) async-start(bf16[16,32,1024]{2,1,0:T(8,128)(2,1)} %broadcast_in_dim.148), calls=%async_computation | async-start | bytes 2097152 | tf_op jit(solution)/shard_map/all_to_all | solution.py:57
  16.2 71.4 %reduce-scatter.3.cloned.1.call-start = ((), (), s32[]{:S(2)}) async-start(), calls=%async_computation.6 | async-start | bytes 2359296 | tf_op jit(solution)/shard_map/reduce_scatter | solution.py:130
  33.9 3.0 collective-permute-start
  35.2 1.2 copy-start.12
  36.8 1.3 copy-start.3
  37.2 1.6 copy-start
  42.5 0.7 copy-start.8
  42.5 47.3 %copy-start.9 = (bf16[8,128,128]{2,1,0:T(8,128)(2,1)S(1)}, bf16[8,128,128]{2,1,0:T(8,128)(2,1)}, u32[]{:S(2)}) copy-start(bf16[8,128,128]{2,1,0:T(8,128)(2,1)} %get-tuple-element.63) | copy-start | bytes 786436
  42.5 86.4 %all-gather.5.cloned.1.call-start = ((), (), s32[]{:S(2)}) async-start(), calls=%async_computation.7 | async-start | bytes 2359296 | tf_op jit(solution)/shard_map/all_gather | solution.py:136
  45.4 3.7 %collective-permute-start.1 = (f32[1025]{0:T(1024)S(1)}, f32[1025]{0:T(1024)S(1)}, u32[]{:S(2)}, u32[]{:S(2)}) collective-permute-start(f32[1025]{0:T(1024)S(1)} %pad_maximum_fusion.3), channel_id=1, source_target_pairs={{0,1},{1,0},{2,3},{3,2},{4,5},{5,4},{6,7},{7,6},{8,9},{9,8},{10,11... | collective-permute-start | bytes 12308 | tf_op jit(solution)/shard_map/ppermute | solution.py:49
  49.8 5.0 %collective-permute-start.2 = (f32[1025]{0:T(1024)S(1)}, f32[1025]{0:T(1024)S(1)}, u32[]{:S(2)}, u32[]{:S(2)}) collective-permute-start(f32[1025]{0:T(1024)S(1)} %fusion.63), channel_id=1, source_target_pairs={{0,2},{1,3},{2,0},{3,1},{4,6},{5,7},{6,4},{7,5},{8,10},{9,11},{10,... | collective-permute-start | bytes 12308 | tf_op jit(solution)/shard_map/ppermute | solution.py:49
  54.8 7.7 %collective-permute-start.3 = (f32[1025]{0:T(1024)S(1)}, f32[1025]{0:T(1024)S(1)}, u32[]{:S(2)}, u32[]{:S(2)}) collective-permute-start(f32[1025]{0:T(1024)S(1)} %add.135), channel_id=1, source_target_pairs={{0,4},{1,5},{2,6},{3,7},{4,0},{5,1},{6,2},{7,3},{8,12},{9,13},{10,... | collective-permute-start | bytes 12308 | tf_op jit(solution)/shard_map/ppermute | solution.py:49
  63.7 1.4 collective-permute-start.4
  66.3 3.7 %collective-permute-start.5 = (f32[1]{0:T(128)}, f32[1]{0:T(128)}, u32[]{:S(2)}, u32[]{:S(2)}) collective-permute-start(f32[1]{0:T(128)} %add.137), channel_id=1, source_target_pairs={{0,16},{8,24},{16,0},{24,8},{32,48},{40,56},{48,32},{56,40},{64,80... | collective-permute-start | bytes 20 | tf_op jit(solution)/shard_map/ppermute | solution.py:49
  70.7 5.2 %collective-permute-start.6 = (f32[1]{0:T(128)}, f32[1]{0:T(128)}, u32[]{:S(2)}, u32[]{:S(2)}) collective-permute-start(f32[1]{0:T(128)} %add.138), channel_id=1, source_target_pairs={{0,32},{8,40},{16,48},{24,56},{32,0},{40,8},{48,16},{56,24},{64,96... | collective-permute-start | bytes 20 | tf_op jit(solution)/shard_map/ppermute | solution.py:49
  76.6 3.7 %collective-permute-start.7 = (f32[1]{0:T(128)}, f32[1]{0:T(128)}, u32[]{:S(2)}, u32[]{:S(2)}) collective-permute-start(f32[1]{0:T(128)} %add.139), channel_id=1, source_target_pairs={{0,64},{8,72},{16,80},{24,88},{32,96},{40,104},{48,112},{56,120},{... | collective-permute-start | bytes 20 | tf_op jit(solution)/shard_map/ppermute | solution.py:49
  80.9 5.2 %collective-permute-start.8 = (f32[1]{0:T(128)}, f32[1]{0:T(128)}, u32[]{:S(2)}, u32[]{:S(2)}) collective-permute-start(f32[1]{0:T(128)} %add.140), channel_id=1, source_target_pairs={{0,128},{8,136},{16,144},{24,152},{32,160},{40,168},{48,176},{56,1... | collective-permute-start | bytes 20 | tf_op jit(solution)/shard_map/ppermute | solution.py:49
  89.5 137.0 %reduce-scatter.5.cloned.1.call-start = ((), (), s32[]{:S(2)}) async-start(), calls=%async_computation.8 | async-start | bytes 2359296 | tf_op jit(solution)/shard_map/reduce_scatter | solution.py:145
  90.4 44.4 %copy-start.5 = (bf16[8,128,8,128]{3,2,1,0:T(8,128)(2,1)}, bf16[8,128,8,128]{3,2,1,0:T(8,128)(2,1)S(1)}, u32[]{:S(2)}) copy-start(bf16[8,128,8,128]{3,2,1,0:T(8,128)(2,1)S(1)} %select_add_fusion) | copy-start | bytes 6291460
  131.8 2.9 collective-permute-start.9
  136.0 24.4 %copy-start.11 = (bf16[32,1024]{1,0:T(8,128)(2,1)S(1)}, bf16[32,1024]{1,0:T(8,128)(2,1)}, u32[]{:S(2)}) copy-start(bf16[32,1024]{1,0:T(8,128)(2,1)} %param.12) | copy-start | bytes 196612
  160.4 22.5 %copy-start.10 = (bf16[32,1024]{1,0:T(8,128)(2,1)}, bf16[32,1024]{1,0:T(8,128)(2,1)S(1)}, u32[]{:S(2)}) copy-start(bf16[32,1024]{1,0:T(8,128)(2,1)S(1)} %reduce_sum.86) | copy-start | bytes 196612
  180.1 2.7 collective-permute-start.10
  183.1 2.3 copy-start.6
  183.4 1.4 copy-start.2
  189.2 1.6 copy-start.1
  189.2 82.7 %all-gather.7.cloned.1.call-start = ((), (), s32[]{:S(2)}) async-start(), calls=%async_computation.9 | async-start | bytes 2506752 | tf_op jit(solution)/shard_map/all_gather | solution.py:156
  193.3 4.1 %copy-start.7 = (bf16[1024,1024]{1,0:T(8,128)(2,1)S(1)}, bf16[1024,1024]{1,0:T(8,128)(2,1)}, u32[]{:S(2)}) copy-start(bf16[1024,1024]{1,0:T(8,128)(2,1)} %copy.100) | copy-start | bytes 6291460
  273.8 1.6 copy-start.4
  277.6 4.4 %collective-permute-start.11 = (bf16[512,1024]{1,0:T(8,128)(2,1)}, bf16[512,1024]{1,0:T(8,128)(2,1)}, u32[]{:S(2)}, u32[]{:S(2)}) collective-permute-start(bf16[512,1024]{1,0:T(8,128)(2,1)} %fusion.27), channel_id=1, source_target_pairs={{0,8},{8,0},{1,9},{9,1},{2,10},{10,2},{3,11},{11,3},{4,12},{12,4},... | collective-permute-start | bytes 3145736 | tf_op jit(solution)/shard_map/ppermute | solution.py:71
  279.1 1.6 collective-permute-start.12
  286.4 28.0 %all-to-all-start.3 = ((bf16[16,33,1024]{2,1,0:T(8,128)(2,1)}), bf16[16,33,1024]{2,1,0:T(8,128)(2,1)S(1)}, u32[]{:S(2)}, u32[]{:S(2)}) async-start(bf16[16,33,1024]{2,1,0:T(8,128)(2,1)} %pad_maximum_fusion.2), calls=%async_computation.5 | async-start | bytes 2621440 | tf_op jit(solution)/shard_map/all_to_all | solution.py:173
Sparse Core Ops, SparseCore 0:
  42.6 40.4 reduce-scatter.2
  89.6 39.2 all-gather.4
  189.3 37.1 reduce-scatter.4
  231.4 40.4 all-gather.6
where the time goes:
time: 326 us; the launch traced here: 324 us
  waiting for transfers between devices  151 us (46%)
  blocking collectives  43.7 us (13%)
  starting transfers between devices  31.9 us (10%)
  local copies, waits for them, and re-layouts  30 us (9%)
  matrix products  24.2 us (7%)
  between operations  22.7 us (7%)
  other arithmetic  21.4 us (7%)
    all_gather x1, waiting for transfers between devices, body(): lax.all_gather(with_row(slope_own, split_three(curvature_part)), 'blk', a...  40.6 us
    all_gather x1, waiting for transfers between devices, body(): active_full = lax.all_gather(active_own, 'blk', axis=0, tiled=True)  38.5 us
    all_to_all x1, blocking collectives, sum_rows(): lax.all_to_all(pair_rows(left, product), 'chip', 0, 0, tiled=False)  24.1 us
    reduce_scatter x1, waiting for transfers between devices, body(): lax.psum_scatter(back_part.astype(jnp.bfloat16), 'blk', scatter_dimension...  23 us
    all_to_all x1, blocking collectives, gather_rows(): mine = lax.all_to_all(spread, 'chip', 0, 0, tiled=False)  19.5 us
    ppermute x8, waiting for transfers between devices, butterfly_sum(): lax.ppermute(value, axis, [(i, i ^ step) for i in range(size)])  18.7 us
    all_to_all x1, waiting for transfers between devices, gather_rows(): mine = lax.all_to_all(spread, 'chip', 0, 0, tiled=False)  17.6 us
    ppermute x8, starting transfers between devices, butterfly_sum(): lax.ppermute(value, axis, [(i, i ^ step) for i in range(size)])  17.1 us
  transfers between devices with their start and end apart: 19, of which 16 were waited for; matrix products, arithmetic and copies ran while one was open for 12% of the time, Pallas kernels for 0%

commit v1 on v0

--- a/solution.py
+++ b/solution.py
@@ -133,7 +133,9 @@
     pre_own, spectral = lax.optimization_barrier((pre_own, spectral))
     hidden_own = pre_own / spectral
     active_own = activate(hidden_own).astype(jnp.bfloat16)
-    active_full = lax.all_gather(active_own, "blk", axis=0, tiled=True)
+    active_full = jnp.concatenate(
+        lax.all_to_all(jnp.stack([active_own] * lax.axis_size("blk")), "blk", 0, 0), axis=0
+    )
     outputs = sum_rows(
         active_full, lambda rows: jnp.dot(rows, w2, preferred_element_type=jnp.float32)
     ).astype(jnp.bfloat16)

time: 326 us -> 341 us (1.046)
  starting transfers between devices: 31.9 us -> 40.3 us
  local copies, waits for them, and re-layouts: 30 us -> 35.3 us
  waiting for transfers between devices: 151 us -> 155 us
    all_to_all x0 -> x1, waiting for transfers between devices: none -> 43.6 us  [body(): lax.all_to_all(jnp.stack([active_own] * lax.axis_size('blk')), 'blk', 0, 0)]
    all_gather x1 -> x0, waiting for transfers between devices: 38.5 us -> none  [body(): active_full = lax.all_gather(active_own, 'blk', axis=0, tiled=True)]
    all_to_all x0 -> x1, starting transfers between devices: none -> 8.42 us  [body(): lax.all_to_all(jnp.stack([active_own] * lax.axis_size('blk')), 'blk', 0, 0)]
    unnamed x34 -> x32, local copies, waits for them, and re-layouts: 9.01 us -> 9.78 us
  transfers between devices with their start and end apart: 19 -> 19, of which waited for: 16 -> 16; matrix products, arithmetic and copies ran while one was open for 12% -> 11% of each run, Pallas kernels for 0% -> 0%
where the time goes in v1:
time: 341 us; the launch traced here: 339 us
  waiting for transfers between devices  155 us (45%)
  blocking collectives  41 us (12%)
  starting transfers between devices  40.3 us (12%)
  local copies, waits for them, and re-layouts  35.3 us (10%)
  matrix products  24.2 us (7%)
  between operations  22.2 us (7%)
  other arithmetic  21.7 us (6%)
    all_to_all x1, waiting for transfers between devices, body(): lax.all_to_all(jnp.stack([active_own] * lax.axis_size('blk')), 'blk', 0, 0)  43.6 us
    all_gather x1, waiting for transfers between devices, body(): lax.all_gather(with_row(slope_own, split_three(curvature_part)), 'blk', a...  40.8 us
    reduce_scatter x1, waiting for transfers between devices, body(): lax.psum_scatter(back_part.astype(jnp.bfloat16), 'blk', scatter_dimension...  21.6 us
    all_to_all x1, blocking collectives, sum_rows(): lax.all_to_all(pair_rows(left, product), 'chip', 0, 0, tiled=False)  21.5 us
    all_to_all x1, blocking collectives, gather_rows(): mine = lax.all_to_all(spread, 'chip', 0, 0, tiled=False)  19.5 us
    ppermute x8, waiting for transfers between devices, butterfly_sum(): lax.ppermute(value, axis, [(i, i ^ step) for i in range(size)])  18.6 us
    all_to_all x1, waiting for transfers between devices, gather_rows(): mine = lax.all_to_all(spread, 'chip', 0, 0, tiled=False)  17.6 us
    ppermute x8, starting transfers between devices, butterfly_sum(): lax.ppermute(value, axis, [(i, i ^ step) for i in range(size)])  17.1 us
  transfers between devices with their start and end apart: 19, of which 16 were waited for; matrix products, arithmetic and copies ran while one was open for 11% of the time, Pallas kernels for 0%

profile of v1, /device:TPU:32, one launch (start us, length us, event | category | flops | bytes accessed | tf_op | source)
XLA Modules:
  0.0 339.3 jit_solution(2097227275110595872)
XLA Ops:
  7.2 1.9 broadcast_in_dim.148
  9.1 7.0 %all-to-all-start = ((bf16[16,32,1024]{2,1,0:T(8,128)(2,1)}), bf16[16,32,1024]{2,1,0:T(8,128)(2,1)S(1)}, u32[]{:S(2)}, u32[]{:S(2)}) async-start(bf16[16,32,1024]{2,1,0:T(8,128)(2,1)} %broadcast_in_dim.148), calls=%async_computation | async-start | bytes 2097152 | tf_op jit(solution)/shard_map/all_to_all | solution.py:57
  16.3 17.6 %all-to-all-done = bf16[16,32,1024]{2,1,0:T(8,128)(2,1)S(1)} async-done(((bf16[16,32,1024]{2,1,0:T(8,128)(2,1)}), bf16[16,32,1024]{2,1,0:T(8,128)(2,1)S(1)}, u32[]{:S(2)}, u32[]{:S(2)}) %all-to-all-start) | async-done | bytes 1048608 | tf_op jit(solution)/shard_map/all_to_all | solution.py:57
  33.9 1.3 bitcast_multiply_fusion
  35.2 0.8 slice_bitcast_fusion.1
  37.2 0.9 copy-done.2
  38.8 3.7 %fusion.12 = bf16[1024,1024]{1,0:T(8,128)(2,1)} fusion(bf16[1024,1024]{1,0:T(8,128)(2,1)S(1)} %bitcast.170, bf16[128,8,8,128]{3,2,1,0:T(8,128)(2,1)S(1)} %bitcast.175), kind=kOutput, calls=%fused_computation.24 | convolution fusion | flops 2148532224 | bytes 6291456 | tf_op jit(solution)/shard_map/dot_general | solution.py:129
  45.5 3.5 %collective-permute-done.1 = f32[1025]{0:T(1024)S(1)} collective-permute-done((f32[1025]{0:T(1024)S(1)}, f32[1025]{0:T(1024)S(1)}, u32[]{:S(2)}, u32[]{:S(2)}) %collective-permute-start.1) | collective-permute-done | bytes 4132 | tf_op jit(solution)/shard_map/ppermute | solution.py:49
  49.7 3.4 collective-permute-start.2
  53.1 1.6 collective-permute-done.2
  54.7 6.0 %collective-permute-start.3 = (f32[1025]{0:T(1024)S(1)}, f32[1025]{0:T(1024)S(1)}, u32[]{:S(2)}, u32[]{:S(2)}) collective-permute-start(f32[1025]{0:T(1024)S(1)} %add.135), channel_id=1, source_target_pairs={{0,4},{1,5},{2,6},{3,7},{4,0},{5,1},{6,2},{7,3},{8,12},{9,13},{10,... | collective-permute-start | bytes 12308 | tf_op jit(solution)/shard_map/ppermute | solution.py:49
  60.8 1.7 collective-permute-done.3
  63.6 1.4 collective-permute-done.4
  66.2 2.0 collective-permute-start.5
  68.2 1.7 collective-permute-done.5
  70.5 2.1 collective-permute-start.6
  72.6 3.1 collective-permute-done.6
  76.3 1.4 collective-permute-start.7
  77.6 2.3 collective-permute-done.7
  80.6 2.0 collective-permute-start.8
  82.5 3.3 collective-permute-done.8
  87.0 1.0 convert_element_type.127
  88.4 1.6 stack.56
  90.0 8.4 %all-to-all-start.1 = ((bf16[8,128,1024]{1,2,0:T(8,128)(2,1)}), bf16[8,128,1024]{1,2,0:T(8,128)(2,1)}, u32[]{:S(2)}, u32[]{:S(2)}) async-start(bf16[8,128,1024]{1,2,0:T(8,128)(2,1)} %stack.56), calls=%async_computation.2 | async-start | bytes 4194304 | tf_op jit(solution)/shard_map/all_to_all | solution.py:137
  98.6 2.0 select_add_fusion
  100.6 43.6 %all-to-all-done.1 = bf16[8,128,1024]{1,2,0:T(8,128)(2,1)} async-done(((bf16[8,128,1024]{1,2,0:T(8,128)(2,1)}), bf16[8,128,1024]{1,2,0:T(8,128)(2,1)}, u32[]{:S(2)}, u32[]{:S(2)}) %all-to-all-start.1) | async-done | bytes 2097184 | tf_op jit(solution)/shard_map/all_to_all | solution.py:137
  144.2 2.9 copy.130
  147.2 1.4 copy-done.4
  148.7 1.2 fusion.33
  150.2 2.6 collective-permute-done.9
  152.9 1.3 add_convert_fusion.1
  154.1 21.5 %all_to_all.25 = bf16[16,32,1024]{2,1,0:T(8,128)(2,1)} all-to-all(bf16[16,32,1024]{2,1,0:T(8,128)(2,1)S(1)} %bitcast.191), channel_id=1, replica_groups=mesh['chip'=16,'core'=2,'blk'=8] {'chip'}, dimensions={0} | all-to-all | bytes 2097152 | tf_op jit(solution)/shard_map/all_to_all | solution.py:78
  175.7 1.4 reduce_sum.86
  177.3 19.5 %all_to_all.26 = bf16[16,32,1024]{2,1,0:T(8,128)(2,1)S(1)} all-to-all(bf16[16,32,1024]{2,1,0:T(8,128)(2,1)S(1)} %broadcast_in_dim.172), channel_id=1, replica_groups=mesh['chip'=16,'core'=2,'blk'=8] {'chip'}, dimensions={0} | all-to-all | bytes 2097152 | tf_op jit(solution)/shard_map/all_to_all | solution.py:57
  196.8 2.7 collective-permute-done.10
  200.0 1.4 copy-done.1
  201.4 0.7 copy-done.5
  202.1 3.7 %fusion.15 = bf16[1024,1024]{1,0:T(8,128)(2,1)} fusion(bf16[1024,1024]{1,0:T(8,128)(2,1)S(1)} %bitcast.172, bf16[128,8,8,128]{3,2,1,0:T(8,128)(2,1)S(1)} %bitcast.180), kind=kOutput, calls=%fused_computation.25 | convolution fusion | flops 2148532224 | bytes 6291456 | tf_op jit(solution)/shard_map/dot_general | solution.py:144
  206.7 2.6 copy.137
  209.3 4.1 %copy.135 = bf16[1024,1024]{1,0:T(8,128)(2,1)} copy(bf16[1024,1024]{0,1:T(8,128)(2,1)} %bitcast.173) | data formatting | bytes 4194304 | tf_op jit(solution)/shard_map/dot_general | solution.py:150
  213.4 4.0 %convolution_bitcast_fusion.1 = f32[8,8,128,128]{3,2,1,0:T(8,128)S(1)} fusion(bf16[8,128,1024,1]{2,1,3,0:T(8,128)(2,1)} %bitcast.183, bf16[8,128,1024,1]{2,1,0,3:T(8,128)(2,1)S(1)} %bitcast.182), kind=kOutput, calls=%fused_computation.4 | convolution fusion | flops 2147483648 | bytes 8388608 | tf_op jit(solution)/shard_map/dot_general | solution.py:150
  217.4 1.0 select_reduce_fusion.1
  218.4 1.1 multiply_bitcast_fusion
  219.5 21.6 %reduce-scatter.5.cloned.1.call-done = bf16[128,1024]{1,0:T(8,128)(2,1)} async-done(((bf16[1024,1024]{1,0:T(8,128)(2,1)}), bf16[128,1024]{1,0:T(8,128)(2,1)}) %reduce-scatter.5.cloned.1.call-update) | async-done | bytes 262160 | tf_op jit(solution)/shard_map/reduce_scatter | solution.py:147
  241.1 1.0 convert_element_type.138
  242.1 1.0 multiply_reduce_fusion
  244.4 0.7 broadcast_select_fusion.5
  245.2 0.7 fusion.54
  245.9 40.8 %all-gather.4.cloned.1.call-done = bf16[8,129,1024]{2,1,0:T(8,128)(2,1)} async-done(((bf16[1,129,1024]{2,1,0:T(8,128)(2,1)}), bf16[8,129,1024]{2,1,0:T(8,128)(2,1)}) %all-gather.4.cloned.1.call-update) | async-done | bytes 2113552 | tf_op jit(solution)/shard_map/all_gather | solution.py:158
  286.7 1.9 slice.145
  288.7 1.4 copy-done.3
  290.2 2.3 fusion.27
  292.4 0.7 slice.148
  294.4 1.1 collective-permute-done.12
  296.9 3.1 add_convert_fusion
  300.1 1.2 pad_maximum_fusion.2
  301.3 6.8 %all-to-all-start.4 = ((bf16[16,33,1024]{2,1,0:T(8,128)(2,1)}), bf16[16,33,1024]{2,1,0:T(8,128)(2,1)S(1)}, u32[]{:S(2)}, u32[]{:S(2)}) async-start(bf16[16,33,1024]{2,1,0:T(8,128)(2,1)} %pad_maximum_fusion.2), calls=%async_computation.6 | async-start | bytes 2621440 | tf_op jit(solution)/shard_map/all_to_all | solution.py:175
  308.1 4.0 %copy.139 = bf16[1024,1024]{1,0:T(8,128)(2,1)} copy(bf16[1024,1024]{0,1:T(8,128)(2,1)} %bitcast.171) | data formatting | bytes 4194304 | tf_op jit(solution)/shard_map/dot_general | solution.py:180
  312.6 2.5 copy.143
  315.1 2.6 copy.140
  317.7 4.6 %convolution_bitcast_fusion = f32[8,8,128,128]{3,2,1,0:T(8,128)S(1)} fusion(bf16[8,128,1024,1]{2,1,3,0:T(8,128)(2,1)} %bitcast.181, bf16[8,128,1024,1]{2,1,0,3:T(8,128)(2,1)} %bitcast.184), kind=kOutput, calls=%fused_computation.3 | convolution fusion | flops 2147483648 | bytes 8388608 | tf_op jit(solution)/shard_map/dot_general | solution.py:180
  322.3 1.0 select_reduce_fusion
  323.3 5.9 %all-to-all-done.4 = bf16[16,33,1024]{2,1,0:T(8,128)(2,1)S(1)} async-done(((bf16[16,33,1024]{2,1,0:T(8,128)(2,1)}), bf16[16,33,1024]{2,1,0:T(8,128)(2,1)S(1)}, u32[]{:S(2)}, u32[]{:S(2)}) %all-to-all-start.4) | async-done | bytes 1081376 | tf_op jit(solution)/shard_map/all_to_all | solution.py:175
  331.5 1.3 subtract_bitcast_fusion
  (85 shorter events, 12.3 us)
Async XLA Ops:
  7.2 9.0 %copy-start.12 = (s32[8,1]{0,1:T(1,128)S(1)}, s32[8,1]{0,1:T(1,128)}, u32[]{:S(2)}) copy-start(s32[8,1]{0,1:T(1,128)} %param.17) | copy-start | bytes 100
  9.1 24.7 %all-to-all-start = ((bf16[16,32,1024]{2,1,0:T(8,128)(2,1)}), bf16[16,32,1024]{2,1,0:T(8,128)(2,1)S(1)}, u32[]{:S(2)}, u32[]{:S(2)}) async-start(bf16[16,32,1024]{2,1,0:T(8,128)(2,1)} %broadcast_in_dim.148), calls=%async_computation | async-start | bytes 2097152 | tf_op jit(solution)/shard_map/all_to_all | solution.py:57
  16.2 70.9 %reduce-scatter.3.cloned.1.call-start = ((), (), s32[]{:S(2)}) async-start(), calls=%async_computation.7 | async-start | bytes 2359296 | tf_op jit(solution)/shard_map/reduce_scatter | solution.py:130
  33.9 3.0 collective-permute-start
  35.2 1.2 copy-start.11
  36.8 1.3 copy-start.2
  37.2 1.6 copy-start
  42.4 0.7 copy-start.7
  45.3 3.7 %collective-permute-start.1 = (f32[1025]{0:T(1024)S(1)}, f32[1025]{0:T(1024)S(1)}, u32[]{:S(2)}, u32[]{:S(2)}) collective-permute-start(f32[1025]{0:T(1024)S(1)} %pad_maximum_fusion.3), channel_id=1, source_target_pairs={{0,1},{1,0},{2,3},{3,2},{4,5},{5,4},{6,7},{7,6},{8,9},{9,8},{10,11... | collective-permute-start | bytes 12308 | tf_op jit(solution)/shard_map/ppermute | solution.py:49
  49.7 5.0 %collective-permute-start.2 = (f32[1025]{0:T(1024)S(1)}, f32[1025]{0:T(1024)S(1)}, u32[]{:S(2)}, u32[]{:S(2)}) collective-permute-start(f32[1025]{0:T(1024)S(1)} %fusion.63), channel_id=1, source_target_pairs={{0,2},{1,3},{2,0},{3,1},{4,6},{5,7},{6,4},{7,5},{8,10},{9,11},{10,... | collective-permute-start | bytes 12308 | tf_op jit(solution)/shard_map/ppermute | solution.py:49
  54.7 7.7 %collective-permute-start.3 = (f32[1025]{0:T(1024)S(1)}, f32[1025]{0:T(1024)S(1)}, u32[]{:S(2)}, u32[]{:S(2)}) collective-permute-start(f32[1025]{0:T(1024)S(1)} %add.135), channel_id=1, source_target_pairs={{0,4},{1,5},{2,6},{3,7},{4,0},{5,1},{6,2},{7,3},{8,12},{9,13},{10,... | collective-permute-start | bytes 12308 | tf_op jit(solution)/shard_map/ppermute | solution.py:49
  63.6 1.4 collective-permute-start.4
  66.2 3.7 %collective-permute-start.5 = (f32[1]{0:T(128)}, f32[1]{0:T(128)}, u32[]{:S(2)}, u32[]{:S(2)}) collective-permute-start(f32[1]{0:T(128)} %add.137), channel_id=1, source_target_pairs={{0,16},{8,24},{16,0},{24,8},{32,48},{40,56},{48,32},{56,40},{64,80... | collective-permute-start | bytes 20 | tf_op jit(solution)/shard_map/ppermute | solution.py:49
  70.5 5.2 %collective-permute-start.6 = (f32[1]{0:T(128)}, f32[1]{0:T(128)}, u32[]{:S(2)}, u32[]{:S(2)}) collective-permute-start(f32[1]{0:T(128)} %add.138), channel_id=1, source_target_pairs={{0,32},{8,40},{16,48},{24,56},{32,0},{40,8},{48,16},{56,24},{64,96... | collective-permute-start | bytes 20 | tf_op jit(solution)/shard_map/ppermute | solution.py:49
  76.3 3.7 %collective-permute-start.7 = (f32[1]{0:T(128)}, f32[1]{0:T(128)}, u32[]{:S(2)}, u32[]{:S(2)}) collective-permute-start(f32[1]{0:T(128)} %add.139), channel_id=1, source_target_pairs={{0,64},{8,72},{16,80},{24,88},{32,96},{40,104},{48,112},{56,120},{... | collective-permute-start | bytes 20 | tf_op jit(solution)/shard_map/ppermute | solution.py:49
  80.6 5.2 %collective-permute-start.8 = (f32[1]{0:T(128)}, f32[1]{0:T(128)}, u32[]{:S(2)}, u32[]{:S(2)}) collective-permute-start(f32[1]{0:T(128)} %add.140), channel_id=1, source_target_pairs={{0,128},{8,136},{16,144},{24,152},{32,160},{40,168},{48,176},{56,1... | collective-permute-start | bytes 20 | tf_op jit(solution)/shard_map/ppermute | solution.py:49
  90.0 8.6 %copy-start.8 = (bf16[8,128,128]{2,1,0:T(8,128)(2,1)S(1)}, bf16[8,128,128]{2,1,0:T(8,128)(2,1)}, u32[]{:S(2)}) copy-start(bf16[8,128,128]{2,1,0:T(8,128)(2,1)} %get-tuple-element.71) | copy-start | bytes 786436
  90.0 54.2 %all-to-all-start.1 = ((bf16[8,128,1024]{1,2,0:T(8,128)(2,1)}), bf16[8,128,1024]{1,2,0:T(8,128)(2,1)}, u32[]{:S(2)}, u32[]{:S(2)}) async-start(bf16[8,128,1024]{1,2,0:T(8,128)(2,1)} %stack.56), calls=%async_computation.2 | async-start | bytes 4194304 | tf_op jit(solution)/shard_map/all_to_all | solution.py:137
  98.5 142.7 %reduce-scatter.5.cloned.1.call-start = ((), (), s32[]{:S(2)}) async-start(), calls=%async_computation.8 | async-start | bytes 2359296 | tf_op jit(solution)/shard_map/reduce_scatter | solution.py:147
  147.1 1.6 copy-start.4
  149.9 2.9 collective-permute-start.9
  154.1 23.0 %copy-start.10 = (bf16[32,1024]{1,0:T(8,128)(2,1)S(1)}, bf16[32,1024]{1,0:T(8,128)(2,1)}, u32[]{:S(2)}) copy-start(bf16[32,1024]{1,0:T(8,128)(2,1)} %param.12) | copy-start | bytes 196612
  177.1 22.5 %copy-start.9 = (bf16[32,1024]{1,0:T(8,128)(2,1)}, bf16[32,1024]{1,0:T(8,128)(2,1)S(1)}, u32[]{:S(2)}) copy-start(bf16[32,1024]{1,0:T(8,128)(2,1)S(1)} %reduce_sum.86) | copy-start | bytes 196612
  196.8 2.7 collective-permute-start.10
  199.8 2.3 copy-start.5
  200.0 1.4 copy-start.1
  205.9 80.8 %all-gather.4.cloned.1.call-start = ((), (), s32[]{:S(2)}) async-start(), calls=%async_computation.9 | async-start | bytes 2506752 | tf_op jit(solution)/shard_map/all_gather | solution.py:158
  209.3 4.1 %copy-start.6 = (bf16[1024,1024]{1,0:T(8,128)(2,1)S(1)}, bf16[1024,1024]{1,0:T(8,128)(2,1)}, u32[]{:S(2)}) copy-start(bf16[1024,1024]{1,0:T(8,128)(2,1)} %copy.137) | copy-start | bytes 6291460
  288.6 1.6 copy-start.3
  292.4 4.4 %collective-permute-start.11 = (bf16[512,1024]{1,0:T(8,128)(2,1)}, bf16[512,1024]{1,0:T(8,128)(2,1)}, u32[]{:S(2)}, u32[]{:S(2)}) collective-permute-start(bf16[512,1024]{1,0:T(8,128)(2,1)} %fusion.27), channel_id=1, source_target_pairs={{0,8},{8,0},{1,9},{9,1},{2,10},{10,2},{3,11},{11,3},{4,12},{12,4},... | collective-permute-start | bytes 3145736 | tf_op jit(solution)/shard_map/ppermute | solution.py:71
  293.9 1.6 collective-permute-start.12
  301.3 28.0 %all-to-all-start.4 = ((bf16[16,33,1024]{2,1,0:T(8,128)(2,1)}), bf16[16,33,1024]{2,1,0:T(8,128)(2,1)S(1)}, u32[]{:S(2)}, u32[]{:S(2)}) async-start(bf16[16,33,1024]{2,1,0:T(8,128)(2,1)} %pad_maximum_fusion.2), calls=%async_computation.6 | async-start | bytes 2621440 | tf_op jit(solution)/shard_map/all_to_all | solution.py:175
Sparse Core Ops, SparseCore 0:
  42.6 40.3 reduce-scatter.2
  206.0 35.0 reduce-scatter.4
  246.0 40.6 all-gather.3
